TPU v7x, 32 devices: a whole 2x2x4 slice. The times are simulated.
32 devices in a mesh: row: 2 (over x), col: 4 (over z), tok: 4 (over y, core).
Axes of the slice: x: 2, y: 2, z: 4, core: 2. Of those that a mesh axis runs over, the one named last changes fastest.
Arguments:
- activations: bfloat16 [4096, 2048], P(('row', 'col', 'tok')), may hold values from -6 to 6
- norm_gain: float32 [2048], replicated, may hold values from 0.1 to 1.9
- routes: int32 [4096, 8], P(('row', 'col', 'tok')), may hold values from 0 to 127, all different within a row; in each aligned block of 128 rows (0 to 127, 128 to 255, ...) at most 10 rows name the same one
- route_weights: float32 [4096, 8], P(('row', 'col', 'tok')), may hold values from 0.05 to 1
- gate_up_weight: bfloat16 [128, 2, 768, 2048], P(('row', 'col'), None, 'tok'), may hold values from -0.125 to 0.125
- down_weight: bfloat16 [128, 768, 2048], P(('row', 'col'), 'tok'), may hold values from -0.21875 to 0.21875
Outputs:
- expert_mix: bfloat16 [4096, 2048], P(('row', 'col', 'tok'))
Inputs may be any that keep to these rules, and one draw needn't show every extreme that they name: `routes`: within the rows of one device no expert is named by more than 10 rows, a bound that some block reaches.
All inputs are finite; a program needn't handle non-finite values.
Results may differ from a plain program's by a relative error of at most 0.0085.
Values may be sent and summed in bfloat16 or wider, within the bound.
No kernel may reach another device: no remote copies, remote signals or barrier semaphores. Data moves between devices by JAX's collectives and lax.ppermute only.
A program may use at most 384 MiB of HBM per device.

v0:
```python
import jax
import jax.numpy as jnp
from jax import lax
from jax.sharding import PartitionSpec as P

CAP = 10
EPSILON = 1e-06
ALL = ("row", "col", "tok")


def rank_in_block(block_routes, experts):
    onehot = (block_routes[:, None] == jnp.arange(experts, dtype=jnp.int32)[None, :]).astype(
        jnp.int32
    )
    before = jnp.cumsum(onehot, axis=0) - onehot
    return jnp.sum(before * onehot, axis=1)


def rms_normed(activations, norm_gain):
    values = activations.astype(jnp.float32)
    scale = lax.rsqrt(jnp.mean(values * values, axis=-1, keepdims=True) + EPSILON)
    return (values * scale * norm_gain).astype(jnp.bfloat16)


def local(activations, norm_gain, routes, route_weights, gate_up_weight, down_weight):
    count, features = activations.shape
    chosen = routes.shape[1]
    holding = gate_up_weight.shape[0]
    row_count = lax.axis_size("row")
    col_count = lax.axis_size("col")
    tok_count = lax.axis_size("tok")
    owners = row_count * col_count
    experts = holding * owners
    devices = owners * tok_count
    owner = lax.axis_index("row") * col_count + lax.axis_index("col")
    normed = rms_normed(activations, norm_gain)
    gates = route_weights / jnp.sum(route_weights, axis=1, keepdims=True)
    flat_routes = routes.reshape(-1)
    target = flat_routes * CAP + rank_in_block(flat_routes, experts)
    every_normed = lax.all_gather(normed, ALL, axis=0, tiled=True)
    every_target = lax.all_gather(target, ALL, axis=0, tiled=False)
    source = jnp.arange(devices, dtype=jnp.int32)[:, None]
    pair = jnp.arange(count * chosen, dtype=jnp.int32)[None, :]
    expert = every_target // CAP
    rank = every_target % CAP
    mine = expert // holding == owner
    slot = (
        (source % tok_count * owners + source // tok_count) * holding + expert % holding
    ) * CAP + rank
    slots = tok_count * owners * holding * CAP
    slot = jnp.where(mine, slot, slots)
    token = source * count + pair // chosen
    table = (
        jnp.full((slots,), devices * count, jnp.int32)
        .at[slot.reshape(-1)]
        .set(token.reshape(-1), mode="drop")
    )
    picked = jnp.take(every_normed, table, axis=0, mode="fill", fill_value=0)
    picked = picked.reshape(tok_count * owners, holding, CAP, features)
    both = jnp.einsum(
        "sjcd,jgfd->sjcgf", picked, gate_up_weight, preferred_element_type=jnp.float32
    )
    hidden = (jax.nn.silu(both[:, :, :, 0, :]) * both[:, :, :, 1, :]).astype(jnp.bfloat16)
    partial = jnp.einsum("sjcf,jfd->sjcd", hidden, down_weight, preferred_element_type=jnp.float32)
    summed = lax.psum_scatter(partial, "tok", scatter_dimension=0, tiled=True)
    results = summed.astype(jnp.bfloat16)
    returned = lax.all_to_all(results, ("row", "col"), split_axis=0, concat_axis=0, tiled=True)
    picked_back = jnp.take(returned.reshape(experts * CAP, features), target, axis=0)
    picked_back = picked_back.reshape(count, chosen, features)
    mixed = jnp.einsum("tk,tkd->td", gates, picked_back.astype(jnp.float32))
    return mixed.astype(jnp.bfloat16)


def solution(mesh):
    in_specs = (
        P(("row", "col", "tok"), None),
        P(),
        P(("row", "col", "tok"), None),
        P(("row", "col", "tok"), None),
        P(("row", "col"), None, "tok", None),
        P(("row", "col"), "tok", None),
    )
    out_specs = P(("row", "col", "tok"), None)
    return jax.shard_map(local, mesh=mesh, in_specs=in_specs, out_specs=out_specs, check_vma=False)
```

profile of v0, /device:TPU:0, one launch (start us, length us, event | category | flops | bytes accessed | tf_op | source)
XLA Modules:
  0.0 799.6 jit_solution(5752293919866283598)
XLA Ops:
  6.5 0.0 all-gather.3.cloned.1.call-start
  6.5 1.2 fusion.16
  7.8 2.0 fusion.18
  9.8 0.0 all-gather.3.cloned.1.call-update
  9.8 0.0 reduce-scatter.2.cloned.1.call-start
  9.9 0.8 copy.47
  10.7 0.1 eq.37
  10.8 0.1 reshape.240
  10.9 0.1 copy.49
  11.0 0.2 fusion.21
  11.3 0.1 copy.50
  11.4 0.7 broadcast_multiply_fusion
  12.1 0.1 copy.53
  12.2 0.1 mul.101
  12.3 0.4 fusion.20
  12.6 0.0 copy-start.2
  12.7 44.2 %all-gather = s32[32,1,1024]{2,1,0:T(1,128)S(1)} all-gather(s32[1,1,1024]{2,1,0:T(1,128)S(1)} %add_bitcast_fusion.1), channel_id=1, replica_groups=mesh['row'=2,'col'=4,'tok'=4] {'row','col','tok'}, dimensions={0}, use_global_device_ids=true | all-gather | bytes 135168 | tf_op jit(solution)/shard_map/all_gather | solution.py:41
  56.9 0.3 broadcast_remainder_fusion
  57.2 0.3 fusion.29
  57.5 0.1 copy.71
  57.6 0.1 add_bitcast_fusion
  57.7 0.1 compare_select_fusion
  57.9 120.3 %scatter_custom_fusion = s32[5120]{0:T(1024)S(1)} fusion(s32[32768]{0:T(1024)S(1)} %bitcast.89, s32[32768]{0:T(1024)S(1)} %bitcast.88, s32[]{:T(128)} %constant.127.clone.1), kind=kCustom, calls=%fused_computation.64 | custom fusion | bytes 20484 | tf_op jit(solution)/shard_map/scatter | solution.py:56
  178.2 0.3 broadcast_in_dim.41
  178.5 0.0 all-gather.3.cloned.1.call-done
  178.5 46.8 %gather_fusion = bf16[5120,2048]{1,0:T(8,128)(2,1)} fusion(bf16[4096,2048]{1,0:T(8,128)(2,1)} %all-gather.3.cloned.1.call-done, s32[5120]{0:T(1024)S(1)} %fusion.35), kind=kCustom, calls=%fused_computation | custom fusion | bytes 41963520 | tf_op jit(solution)/shard_map/jit(_take)/gather | solution.py:58
  225.3 0.0 copy-done
  225.3 34.0 %gather.13 = bf16[32,16,10,2048]{3,2,1,0:T(8,128)(2,1)} reshape(bf16[5120,2048]{1,0:T(8,128)(2,1)} %gather_fusion) | data formatting | bytes 41943040 | tf_op jit(solution)/shard_map/jit(_take)/gather | solution.py:58
  259.3 22.7 %select_bitcast_fusion = bf16[32,16,10,2048,1]{3,2,1,0,4:T(8,128)(2,1)} fusion(bf16[32,16,10,2048]{3,2,1,0:T(8,128)(2,1)} %gather.13, pred[32,16,10]{2,1,0:T(8,128)(4,1)S(1)} %broadcast_in_dim.41), kind=kLoop, calls=%fused_computation.3 | loop fusion | flops 10485760 | bytes 41948160 | tf_op jit(solution)/shard_map/jit(_take)/select_n | solution.py:58
  282.1 34.1 %fusion.8 = f32[32,16,10,2,192]{4,0,3,2,1:T(8,128)} fusion(bf16[16,2,192,2048]{3,2,1,0:T(8,128)(2,1)} %param.10, bf16[32,16,10,2048,1]{3,2,1,0,4:T(8,128)(2,1)} %select_bitcast_fusion), kind=kOutput, calls=%fused_computation.16 | convolution fusion | flops 8053063680 | bytes 54001664 | tf_op jit(solution)/shard_map/sjcd,jgfd->sjcgf/dot_general | solution.py:60
  316.2 22.9 %convolution_bitcast_fusion = f32[32,16,10,2048]{3,0,2,1:T(8,128)} fusion(bf16[16,192,2048]{2,1,0:T(8,128)(2,1)} %param.11, f32[32,16,10,2,192]{4,0,3,2,1:T(8,128)} %fusion.8), kind=kOutput, calls=%fused_computation.7 | convolution fusion | flops 4032430080 | bytes 62390272 | tf_op jit(solution)/shard_map/sjcf,jfd->sjcd/dot_general | solution.py:64
  339.0 0.0 reduce-scatter.2.cloned.1.call-update
  339.0 285.4 %reduce-scatter.2.cloned.1.call-done = f32[8,16,10,2048]{3,0,2,1:T(8,128)} async-done(((f32[32,16,10,2048]{3,0,2,1:T(8,128)}), f32[8,16,10,2048]{3,0,2,1:T(8,128)}) %reduce-scatter.2.cloned.1.call-update) | async-done | bytes 10485776 | tf_op jit(solution)/shard_map/reduce_scatter | solution.py:65
  624.4 4.8 convert_element_type.28
  629.2 0.0 copy-start.4
  629.2 0.0 copy-start.5
  629.2 5.2 copy.59
  634.4 5.5 all-to-all-start
  639.9 0.1 mul.117
  640.0 0.1 reduce_sum.35
  640.2 0.1 copy.52
  640.4 0.1 copy.65
  640.5 116.0 %all-to-all-done = bf16[8,16,10,2048]{3,1,2,0:T(8,128)(2,1)} async-done(((bf16[8,16,10,2048]{3,1,2,0:T(8,128)(2,1)}), bf16[8,16,10,2048]{3,1,2,0:T(8,128)(2,1)}, u32[]{:S(2)}, u32[]{:S(2)}) %all-to-all-start) | async-done | bytes 5242912 | tf_op jit(solution)/shard_map/all_to_all | solution.py:67
  756.6 9.7 %copy.60 = bf16[8,16,10,2048]{3,2,1,0:T(8,128)(2,1)} copy(bf16[8,16,10,2048]{3,1,2,0:T(8,128)(2,1)} %all-to-all-done) | data formatting | bytes 10485760 | tf_op jit(solution)/shard_map/all_to_all | solution.py:67
  766.3 9.8 %reshape.243 = bf16[1280,2048]{1,0:T(8,128)(2,1)} reshape(bf16[8,16,10,2048]{3,2,1,0:T(8,128)(2,1)} %copy.60) | data formatting | bytes 10485760 | tf_op jit(solution)/shard_map/reshape | solution.py:68
  776.1 12.0 %gather_fusion.1 = bf16[1024,2048]{1,0:T(8,128)(2,1)} fusion(bf16[1280,2048]{1,0:T(8,128)(2,1)} %reshape.243, s32[1024]{0:T(1024)S(1)} %broadcast_clamp_fusion), kind=kCustom, calls=%fused_computation.1 | custom fusion | bytes 8392704 | tf_op jit(solution)/shard_map/jit(_take)/gather | solution.py:68
  788.1 3.5 fusion.6
  791.6 1.1 copy.82
  (26 shorter events, 0.3 us)
Async XLA Ops:
  6.5 172.0 %all-gather.3.cloned.1.call-start = ((), (), s32[]{:S(2)}) async-start(), calls=%async_computation.2 | async-start | bytes 17301504 | tf_op jit(solution)/shard_map/all_gather | solution.py:40
  9.8 614.6 %reduce-scatter.2.cloned.1.call-start = ((), (), s32[]{:S(2)}) async-start(), calls=%async_computation.3 | async-start | bytes 52428800 | tf_op jit(solution)/shard_map/reduce_scatter | solution.py:65
  12.2 213.1 %copy-start = (s32[128,8]{1,0:T(8,128)}, s32[128,8]{1,0:T(8,128)S(1)}, u32[]{:S(2)}) copy-start(s32[128,8]{1,0:T(8,128)S(1)} %copy.53) | copy-start | bytes 12292
  12.6 45.3 %copy-start.2 = (s32[1024]{0:T(1024)}, s32[1024]{0:T(1024)S(1)}, u32[]{:S(2)}) copy-start(s32[1024]{0:T(1024)S(1)} %fusion.20) | copy-start | bytes 12292
  629.2 10.7 %copy-start.1 = (s32[128,8]{1,0:T(8,128)S(1)}, s32[128,8]{1,0:T(8,128)}, u32[]{:S(2)}) copy-start(s32[128,8]{1,0:T(8,128)} %copy-done) | copy-start | bytes 12292
  629.2 10.8 %copy-start.3 = (s32[1024]{0:T(1024)S(1)}, s32[1024]{0:T(1024)}, u32[]{:S(2)}) copy-start(s32[1024]{0:T(1024)} %copy-done.2) | copy-start | bytes 12292
  629.2 11.0 %copy-start.4 = (s32[128,8]{0,1:T(8,128)S(1)}, s32[128,8]{0,1:T(8,128)}, u32[]{:S(2)}) copy-start(s32[128,8]{0,1:T(8,128)} %param.8) | copy-start | bytes 12292
  629.2 11.1 %copy-start.5 = (f32[128,8]{0,1:T(8,128)S(1)}, f32[128,8]{0,1:T(8,128)}, u32[]{:S(2)}) copy-start(f32[128,8]{0,1:T(8,128)} %param.9) | copy-start | bytes 12292
  634.4 122.1 %all-to-all-start = ((bf16[8,16,10,2048]{3,1,2,0:T(8,128)(2,1)}), bf16[8,16,10,2048]{3,1,2,0:T(8,128)(2,1)}, u32[]{:S(2)}, u32[]{:S(2)}) async-start(bf16[8,16,10,2048]{3,1,2,0:T(8,128)(2,1)} %copy.59), calls=%async_computation.1 | async-start | bytes 10485760 | tf_op jit(solution)/shard_map/all_to_all | solution.py:67
Sparse Core Ops, SparseCore 0:
  10.2 117.7 all-gather.2
  339.1 285.1 reduce-scatter.1
where the time goes:
time: 801 us; the launch traced here: 800 us
  waiting for transfers between devices  401 us (50%)
  local copies, waits for them, and re-layouts  241 us (30%)
  matrix products  60.4 us (8%)
  blocking collectives  44.2 us (6%)
  other arithmetic  33 us (4%)
  between operations  13.7 us (2%)
    reduce_scatter x1, waiting for transfers between devices, local(): summed = lax.psum_scatter(partial, 'tok', scatter_dimension=0, tiled=True)  285 us
    scatter x1, local copies, waits for them, and re-layouts, local(): table = jnp.full((slots,), devices * count, jnp.int32).at[slot.reshape(-1...  120 us
    all_to_all x1, waiting for transfers between devices, local(): lax.all_to_all(results, ('row', 'col'), split_axis=0, concat_axis=0, tile...  116 us
    gather x2, local copies, waits for them, and re-layouts, local(): picked = jnp.take(every_normed, table, axis=0, mode='fill', fill_value=0)  80.8 us
    all_gather x1, blocking collectives, local(): every_target = lax.all_gather(target, ALL, axis=0, tiled=False)  44.2 us
    dot_general x1, matrix products, local(): jnp.einsum('sjcd,jgfd->sjcgf', picked, gate_up_weight, preferred_element_...  34.1 us
    dot_general x1, matrix products, local(): jnp.einsum('sjcf,jfd->sjcd', hidden, down_weight, preferred_element_type=...  22.9 us
    select_n x1, other arithmetic, local(): picked = jnp.take(every_normed, table, axis=0, mode='fill', fill_value=0)  22.7 us
  transfers between devices with their start and end apart: 3, of which 2 were waited for; matrix products, arithmetic and copies ran while one was open for 16% of the time, Pallas kernels for 0%

commit v1 on v0

--- a/solution.py
+++ b/solution.py
@@ -64,7 +64,15 @@
     partial = jnp.einsum("sjcf,jfd->sjcd", hidden, down_weight, preferred_element_type=jnp.float32)
     summed = lax.psum_scatter(partial, "tok", scatter_dimension=0, tiled=True)
     results = summed.astype(jnp.bfloat16)
-    returned = lax.all_to_all(results, ("row", "col"), split_axis=0, concat_axis=0, tiled=True)
+    ways, here = (lax.axis_size(("row", "col")), lax.axis_index(("row", "col")))
+    width = results.shape[0] // ways
+    turned = jnp.roll(results, -here * width, axis=0)
+    got = [lax.slice_in_dim(turned, 0, width, axis=0)]
+    for far in range(1, ways):
+        sent = lax.slice_in_dim(turned, far * width, (far + 1) * width, axis=0)
+        got.append(lax.ppermute(sent, ("row", "col"), [(d, (d + far) % ways) for d in range(ways)]))
+    line = jnp.concatenate(got[::-1], axis=0)
+    returned = jnp.roll(line, (here + 1) * got[0].shape[0], axis=0)
     picked_back = jnp.take(returned.reshape(experts * CAP, features), target, axis=0)
     picked_back = picked_back.reshape(count, chosen, features)
     mixed = jnp.einsum("tk,tkd->td", gates, picked_back.astype(jnp.float32))

time: 801 us -> 855 us (1.067)
  local copies, waits for them, and re-layouts: 241 us -> 310 us
  waiting for transfers between devices: 401 us -> 363 us
  other arithmetic: 33 us -> 44.3 us
    all_to_all x1 -> x0, waiting for transfers between devices: 116 us -> none  [local(): lax.all_to_all(results, ('row', 'col'), split_axis=0, concat_axis=0, tile...]
    ppermute x0 -> x7, waiting for transfers between devices: none -> 77.1 us  [local(): lax.ppermute(sent, ('row', 'col'), [(d, (d + far) % ways) for d in range(...]
    slice x0 -> x8, local copies, waits for them, and re-layouts: none -> 28.1 us  [the longest x7 14.8 us: local(): sent = lax.slice_in_dim(turned, far * width, (far + 1) * width, axis=0)]
    concatenate x0 -> x1, local copies, waits for them, and re-layouts: none -> 27.1 us  [local(): line = jnp.concatenate(got[::-1], axis=0)]
    ppermute x0 -> x7, local copies, waits for them, and re-layouts: none -> 22 us  [local(): lax.ppermute(sent, ('row', 'col'), [(d, (d + far) % ways) for d in range(...]
    concatenate x0 -> x2, other arithmetic: none -> 11.3 us  [the longest x1 7.74 us: local(): returned = jnp.roll(line, (here + 1) * got[0].shape[0], axis=0)]
    ppermute x0 -> x7, starting transfers between devices: none -> 10.9 us  [local(): lax.ppermute(sent, ('row', 'col'), [(d, (d + far) % ways) for d in range(...]
    all_to_all x1 -> x0, local copies, waits for them, and re-layouts: 9.73 us -> none  [local(): lax.all_to_all(results, ('row', 'col'), split_axis=0, concat_axis=0, tile...]
  transfers between devices with their start and end apart: 3 -> 9, of which waited for: 2 -> 3; matrix products, arithmetic and copies ran while one was open for 16% -> 19% of each run, Pallas kernels for 0% -> 0%
where the time goes in v1:
time: 855 us; the launch traced here: 847 us
  waiting for transfers between devices  363 us (42%)
  local copies, waits for them, and re-layouts  310 us (36%)
  matrix products  60.6 us (7%)
  other arithmetic  44.3 us (5%)
  blocking collectives  44.1 us (5%)
  between operations  14 us (2%)
  starting transfers between devices  11 us (1%)
    reduce_scatter x1, waiting for transfers between devices, local(): summed = lax.psum_scatter(partial, 'tok', scatter_dimension=0, tiled=True)  285 us
    scatter x1, local copies, waits for them, and re-layouts, local(): table = jnp.full((slots,), devices * count, jnp.int32).at[slot.reshape(-1...  121 us
    gather x2, local copies, waits for them, and re-layouts, local(): picked = jnp.take(every_normed, table, axis=0, mode='fill', fill_value=0)  80.8 us
    ppermute x7, waiting for transfers between devices, local(): lax.ppermute(sent, ('row', 'col'), [(d, (d + far) % ways) for d in range(...  77.1 us
    all_gather x1, blocking collectives, local(): every_target = lax.all_gather(target, ALL, axis=0, tiled=False)  44.1 us
    dot_general x1, matrix products, local(): jnp.einsum('sjcd,jgfd->sjcgf', picked, gate_up_weight, preferred_element_...  34.1 us
    concatenate x1, local copies, waits for them, and re-layouts, local(): line = jnp.concatenate(got[::-1], axis=0)  27.1 us
    dot_general x1, matrix products, local(): jnp.einsum('sjcf,jfd->sjcd', hidden, down_weight, preferred_element_type=...  23 us
  transfers between devices with their start and end apart: 9, of which 3 were waited for; matrix products, arithmetic and copies ran while one was open for 19% of the time, Pallas kernels for 0%

profile of v1, /device:TPU:0, one launch (start us, length us, event | category | flops | bytes accessed | tf_op | source)
XLA Modules:
  0.0 847.0 jit_solution(10397194664405446235)
XLA Ops:
  6.5 1.2 fusion.18
  7.8 2.0 fusion.20
  9.9 0.8 copy.49
  11.0 0.2 fusion.23
  11.4 0.7 broadcast_multiply_fusion
  12.3 0.4 fusion.22
  12.7 44.1 %all-gather = s32[32,1,1024]{2,1,0:T(1,128)S(1)} all-gather(s32[1,1,1024]{2,1,0:T(1,128)S(1)} %add_bitcast_fusion.1), channel_id=1, replica_groups=mesh['row'=2,'col'=4,'tok'=4] {'row','col','tok'}, dimensions={0}, use_global_device_ids=true | all-gather | bytes 135168 | tf_op jit(solution)/shard_map/all_gather | solution.py:41
  56.8 0.3 broadcast_remainder_fusion
  57.1 0.3 fusion.31
  57.8 120.6 %scatter_custom_fusion = s32[5120]{0:T(1024)S(1)} fusion(s32[32768]{0:T(1024)S(1)} %bitcast.89, s32[32768]{0:T(1024)S(1)} %bitcast.88, s32[]{:T(128)} %constant.145.clone.1), kind=kCustom, calls=%fused_computation.70 | custom fusion | bytes 20484 | tf_op jit(solution)/shard_map/scatter | solution.py:56
  178.4 0.3 broadcast_in_dim.41
  178.7 46.8 %gather_fusion = bf16[5120,2048]{1,0:T(8,128)(2,1)} fusion(bf16[4096,2048]{1,0:T(8,128)(2,1)} %all-gather.3.cloned.1.call-done, s32[5120]{0:T(1024)S(1)} %fusion.37), kind=kCustom, calls=%fused_computation | custom fusion | bytes 41963520 | tf_op jit(solution)/shard_map/jit(_take)/gather | solution.py:58
  225.5 34.0 %gather.13 = bf16[32,16,10,2048]{3,2,1,0:T(8,128)(2,1)} reshape(bf16[5120,2048]{1,0:T(8,128)(2,1)} %gather_fusion) | data formatting | bytes 41943040 | tf_op jit(solution)/shard_map/jit(_take)/gather | solution.py:58
  259.5 22.7 %select_bitcast_fusion = bf16[32,16,10,2048,1]{3,2,1,0,4:T(8,128)(2,1)} fusion(bf16[32,16,10,2048]{3,2,1,0:T(8,128)(2,1)} %gather.13, pred[32,16,10]{2,1,0:T(8,128)(4,1)S(1)} %broadcast_in_dim.41), kind=kLoop, calls=%fused_computation.3 | loop fusion | flops 10485760 | bytes 41948160 | tf_op jit(solution)/shard_map/jit(_take)/select_n | solution.py:58
  282.3 34.1 %fusion.10 = f32[32,16,10,2,192]{4,0,3,2,1:T(8,128)} fusion(bf16[16,2,192,2048]{3,2,1,0:T(8,128)(2,1)} %param.12, bf16[32,16,10,2048,1]{3,2,1,0,4:T(8,128)(2,1)} %select_bitcast_fusion), kind=kOutput, calls=%fused_computation.22 | convolution fusion | flops 8053063680 | bytes 54001664 | tf_op jit(solution)/shard_map/sjcd,jgfd->sjcgf/dot_general | solution.py:60
  316.3 23.0 %convolution_bitcast_fusion = f32[32,16,10,2048]{3,0,2,1:T(8,128)} fusion(bf16[16,192,2048]{2,1,0:T(8,128)(2,1)} %param.13, f32[32,16,10,2,192]{4,0,3,2,1:T(8,128)} %fusion.10), kind=kOutput, calls=%fused_computation.7 | convolution fusion | flops 4032430080 | bytes 62390272 | tf_op jit(solution)/shard_map/sjcf,jfd->sjcd/dot_general | solution.py:64
  339.4 285.4 %reduce-scatter.2.cloned.1.call-done = f32[8,16,10,2048]{3,0,2,1:T(8,128)} async-done(((f32[32,16,10,2048]{3,0,2,1:T(8,128)}), f32[8,16,10,2048]{3,0,2,1:T(8,128)}) %reduce-scatter.2.cloned.1.call-update) | async-done | bytes 10485776 | tf_op jit(solution)/shard_map/reduce_scatter | solution.py:65
  624.8 4.8 convert_element_type.28
  629.6 3.6 fusion.5
  633.2 13.3 %fusion.48 = (bf16[1,16,10,2048]{3,0,2,1:T(2,128)(2,1)}, bf16[1,16,10,2048]{3,0,2,1:T(2,128)(2,1)S(1)}, bf16[1,16,10,2048]{3,0,2,1:T(2,128)(2,1)S(1)}, bf16[1,16...) fusion(bf16[8,16,10,2048]{3,0,2,1:T(8,128)(2,1)S(1)} %fusion.5), kind=kLoop, calls=%fused_computation.97 | loop fusion | bytes 10485760 | tf_op jit(solution)/shard_map/slice | solution.py:70
  646.6 1.6 copy.61
  648.1 4.4 collective-permute-start
  652.5 1.6 copy.62
  654.5 2.9 copy.63
  657.3 1.1 collective-permute-start.2
  658.4 2.9 copy.64
  661.3 1.5 collective-permute-start.3
  662.8 2.9 copy.65
  665.6 2.0 collective-permute-start.4
  667.6 1.6 copy.66
  669.2 1.6 copy.67
  670.7 2.0 collective-permute-start.5
  672.8 37.7 %collective-permute-done.1 = bf16[1,16,10,2048]{3,1,2,0:T(8,128)(2,1)} collective-permute-done((bf16[1,16,10,2048]{3,1,2,0:T(8,128)(2,1)}, bf16[1,16,10,2048]{3,1,2,0:T(8,128)(2,1)}, u32[]{:S(2)}, u32[]{:S(2)}) %collective-permute-start.1) | collective-permute-done | bytes 655392 | tf_op jit(solution)/shard_map/ppermute | solution.py:73
  710.6 1.3 copy.68
  711.9 3.5 copy.69
  715.3 3.5 copy.70
  718.9 3.5 copy.71
  722.4 3.4 copy.72
  725.8 39.4 %collective-permute-done.5 = bf16[1,16,10,2048]{3,1,2,0:T(8,128)(2,1)} collective-permute-done((bf16[1,16,10,2048]{3,1,2,0:T(8,128)(2,1)}, bf16[1,16,10,2048]{3,1,2,0:T(8,128)(2,1)}, u32[]{:S(2)}, u32[]{:S(2)}) %collective-permute-start.5) | collective-permute-done | bytes 655392 | tf_op jit(solution)/shard_map/ppermute | solution.py:73
  765.2 3.4 copy.73
  768.6 3.5 copy.74
  772.1 27.1 %concatenate.6 = bf16[8,16,10,2048]{3,0,2,1:T(8,128)(2,1)} concatenate(bf16[1,16,10,2048]{3,0,2,1:T(2,128)(2,1)S(1)} %copy.68, bf16[1,16,10,2048]{3,0,2,1:T(2,128)(2,1)} %copy.69, bf16[1,16,10,2048]{3,0,2,1:T(2,128)(2,1)} %copy.70, bf16[1,16,10,2048]{3,0,2,1:T(2,128)(2,1)} %copy.71, bf16[1,16,10,2048]{3,0,2,1:T(2,128)(2,1)} %copy.72, bf16[1,16,10,2048]{3,0,2,1:T(2,128)(2,1)} %copy.73, ...), dimensions={0} | concatenate | bytes 10485760 | tf_op jit(solution)/shard_map/concatenate | solution.py:74
  799.2 7.7 fusion.4
  807.0 6.5 copy.75
  813.5 9.8 %reshape.243 = bf16[1280,2048]{1,0:T(8,128)(2,1)} reshape(bf16[8,16,10,2048]{3,2,1,0:T(8,128)(2,1)} %copy.75) | data formatting | bytes 10485760 | tf_op jit(solution)/shard_map/reshape | solution.py:76
  823.3 12.0 %gather_fusion.1 = bf16[1024,2048]{1,0:T(8,128)(2,1)} fusion(bf16[1280,2048]{1,0:T(8,128)(2,1)} %reshape.243, s32[1024]{0:T(1024)S(1)} %broadcast_clamp_fusion), kind=kCustom, calls=%fused_computation.1 | custom fusion | bytes 8392704 | tf_op jit(solution)/shard_map/jit(_take)/gather | solution.py:76
  835.3 3.5 fusion.8
  838.8 1.1 copy.97
  (57 shorter events, 1.8 us)
Async XLA Ops:
  6.5 172.2 %all-gather.3.cloned.1.call-start = ((), (), s32[]{:S(2)}) async-start(), calls=%async_computation.1 | async-start | bytes 17301504 | tf_op jit(solution)/shard_map/all_gather | solution.py:40
  9.8 615.0 %reduce-scatter.2.cloned.1.call-start = ((), (), s32[]{:S(2)}) async-start(), calls=%async_computation.2 | async-start | bytes 52428800 | tf_op jit(solution)/shard_map/reduce_scatter | solution.py:65
  12.2 213.3 %copy-start.1 = (s32[128,8]{1,0:T(8,128)}, s32[128,8]{1,0:T(8,128)S(1)}, u32[]{:S(2)}) copy-start(s32[128,8]{1,0:T(8,128)S(1)} %copy.55) | copy-start | bytes 12292
  12.6 45.2 %copy-start.3 = (s32[1024]{0:T(1024)}, s32[1024]{0:T(1024)S(1)}, u32[]{:S(2)}) copy-start(s32[1024]{0:T(1024)S(1)} %fusion.22) | copy-start | bytes 12292
  633.2 20.8 %copy-start.2 = (s32[128,8]{1,0:T(8,128)S(1)}, s32[128,8]{1,0:T(8,128)}, u32[]{:S(2)}) copy-start(s32[128,8]{1,0:T(8,128)} %copy-done.1) | copy-start | bytes 12292
  633.2 20.9 %copy-start.4 = (s32[1024]{0:T(1024)S(1)}, s32[1024]{0:T(1024)}, u32[]{:S(2)}) copy-start(s32[1024]{0:T(1024)} %copy-done.3) | copy-start | bytes 12292
  633.2 21.1 %copy-start.5 = (s32[128,8]{0,1:T(8,128)S(1)}, s32[128,8]{0,1:T(8,128)}, u32[]{:S(2)}) copy-start(s32[128,8]{0,1:T(8,128)} %param.10) | copy-start | bytes 12292
  633.2 21.2 %copy-start.6 = (f32[128,8]{0,1:T(8,128)S(1)}, f32[128,8]{0,1:T(8,128)}, u32[]{:S(2)}) copy-start(f32[128,8]{0,1:T(8,128)} %param.11) | copy-start | bytes 12292
  648.1 22.6 %collective-permute-start = (bf16[1,16,10,2048]{3,1,2,0:T(8,128)(2,1)}, bf16[1,16,10,2048]{3,1,2,0:T(8,128)(2,1)S(1)}, u32[]{:S(2)}, u32[]{:S(2)}) collective-permute-start(bf16[1,16,10,2048]{3,1,2,0:T(8,128)(2,1)} %copy.61), channel_id=1, source_target_pairs={{0,28},{4,0},{8,4},{12,8},{16,12},{20,16},{24,20},{28,24},{1,29},{... | collective-permute-start | bytes 1966088 | tf_op jit(solution)/shard_map/ppermute | solution.py:73
  654.0 56.4 %collective-permute-start.1 = (bf16[1,16,10,2048]{3,1,2,0:T(8,128)(2,1)}, bf16[1,16,10,2048]{3,1,2,0:T(8,128)(2,1)}, u32[]{:S(2)}, u32[]{:S(2)}) collective-permute-start(bf16[1,16,10,2048]{3,1,2,0:T(8,128)(2,1)} %copy.62), channel_id=1, source_target_pairs={{0,24},{4,28},{8,0},{12,4},{16,8},{20,12},{24,16},{28,20},{1,25},{... | collective-permute-start | bytes 1966088 | tf_op jit(solution)/shard_map/ppermute | solution.py:73
  657.3 58.0 %collective-permute-start.2 = (bf16[1,16,10,2048]{3,1,2,0:T(8,128)(2,1)}, bf16[1,16,10,2048]{3,1,2,0:T(8,128)(2,1)}, u32[]{:S(2)}, u32[]{:S(2)}) collective-permute-start(bf16[1,16,10,2048]{3,1,2,0:T(8,128)(2,1)} %copy.63), channel_id=1, source_target_pairs={{0,20},{4,24},{8,28},{12,0},{16,4},{20,8},{24,12},{28,16},{1,21},{... | collective-permute-start | bytes 1966088 | tf_op jit(solution)/shard_map/ppermute | solution.py:73
  661.3 57.6 %collective-permute-start.3 = (bf16[1,16,10,2048]{3,1,2,0:T(8,128)(2,1)}, bf16[1,16,10,2048]{3,1,2,0:T(8,128)(2,1)}, u32[]{:S(2)}, u32[]{:S(2)}) collective-permute-start(bf16[1,16,10,2048]{3,1,2,0:T(8,128)(2,1)} %copy.64), channel_id=1, source_target_pairs={{0,16},{4,20},{8,24},{12,28},{16,0},{20,4},{24,8},{28,12},{1,17},{... | collective-permute-start | bytes 1966088 | tf_op jit(solution)/shard_map/ppermute | solution.py:73
  665.6 56.7 %collective-permute-start.4 = (bf16[1,16,10,2048]{3,1,2,0:T(8,128)(2,1)}, bf16[1,16,10,2048]{3,1,2,0:T(8,128)(2,1)}, u32[]{:S(2)}, u32[]{:S(2)}) collective-permute-start(bf16[1,16,10,2048]{3,1,2,0:T(8,128)(2,1)} %copy.65), channel_id=1, source_target_pairs={{0,12},{4,16},{8,20},{12,24},{16,28},{20,0},{24,4},{28,8},{1,13},{... | collective-permute-start | bytes 1966088 | tf_op jit(solution)/shard_map/ppermute | solution.py:73
  670.7 94.5 %collective-permute-start.5 = (bf16[1,16,10,2048]{3,1,2,0:T(8,128)(2,1)}, bf16[1,16,10,2048]{3,1,2,0:T(8,128)(2,1)}, u32[]{:S(2)}, u32[]{:S(2)}) collective-permute-start(bf16[1,16,10,2048]{3,1,2,0:T(8,128)(2,1)} %copy.66), channel_id=1, source_target_pairs={{0,8},{4,12},{8,16},{12,20},{16,24},{20,28},{24,0},{28,4},{1,9},{5... | collective-permute-start | bytes 1966088 | tf_op jit(solution)/shard_map/ppermute | solution.py:73
  710.4 58.2 %collective-permute-start.6 = (bf16[1,16,10,2048]{3,1,2,0:T(8,128)(2,1)}, bf16[1,16,10,2048]{3,1,2,0:T(8,128)(2,1)}, u32[]{:S(2)}, u32[]{:S(2)}) collective-permute-start(bf16[1,16,10,2048]{3,1,2,0:T(8,128)(2,1)} %copy.67), channel_id=1, source_target_pairs={{0,4},{4,8},{8,12},{12,16},{16,20},{20,24},{24,28},{28,0},{1,5},{5... | collective-permute-start | bytes 1966088 | tf_op jit(solution)/shard_map/ppermute | solution.py:73
  715.3 56.8 %copy-start = (bf16[1,16,10,2048]{3,0,2,1:T(2,128)(2,1)S(1)}, bf16[1,16,10,2048]{3,0,2,1:T(2,128)(2,1)}, u32[]{:S(2)}) copy-start(bf16[1,16,10,2048]{3,0,2,1:T(2,128)(2,1)} %get-tuple-element.6) | copy-start | bytes 1966084
Sparse Core Ops, SparseCore 0:
  10.2 117.7 all-gather.2
  339.5 285.2 reduce-scatter.1
